TPU v7x, 512 devices: a whole 4x8x8 slice. The times are simulated.
512 devices in a mesh: gx: 32 (over x, z), gy: 16 (over y, core).
Axes of the slice: x: 4, y: 8, z: 8, core: 2. Of those that a mesh axis runs over, the one named last changes fastest.
Arguments:
- start_disp: float32 [6, 3, 128, 128, 128], P(None, None, 'gx', 'gy'), may hold values from -6 to 6
- bone_mask: int32 [128, 128, 128], P('gx', 'gy'), may hold values from 0 to 1, as said below
- density: float32 [128, 128, 128], P('gx', 'gy'), may hold values from 0.3 to 1
- load_nodes: int32 [32, 16, 6, 32], P('gx', 'gy'), may hold values from 0 to 31
- load_forces: float32 [32, 16, 6, 3, 32], P('gx', 'gy'), may hold values from -12 to 12
Outputs:
- displacement: float32 [6, 3, 128, 128, 128], P(None, None, 'gx', 'gy')
- new_density: float32 [128, 128, 128], P('gx', 'gy')
Inputs may be any that keep to these rules, and one draw needn't show every extreme that they name: `bone_mask`: 1 marks a bone voxel.
All inputs are finite; a program needn't handle non-finite values.
Results may differ from a plain program's by a relative error of at most 0.0001.
Values sent between devices are 32-bit elements; how exact they have to be, the bound alone decides.
No kernel may reach another device: no remote copies, remote signals or barrier semaphores. Data moves between devices by JAX's collectives and lax.ppermute only.
A program may use at most 64 MiB of HBM per device.

v0:
```python
import jax
import jax.numpy as jnp
import numpy as np
from jax import lax
from jax.sharding import PartitionSpec as P

spring = 0.1
poisson = 0.3
blur_sigma = 2.0
density_cap = 1.0
mean_eps = 1e-06
highest = lax.Precision.HIGHEST


def from_behind(block, axis, distance):
    devices = range(lax.axis_size(axis))
    route = [(i - distance, i) for i in devices if i - distance in devices]
    return lax.ppermute(block, axis, route)


def with_halo(cells, sides, width):
    for axis, dim in sides:
        count = lax.axis_size(axis)
        ends = count - 1
        head = lax.slice_in_dim(cells, 0, width, axis=dim)
        tail = lax.slice_in_dim(cells, cells.shape[dim] - width, cells.shape[dim], axis=dim)
        cells = jnp.concatenate(
            [
                lax.ppermute(tail, axis, [(i, (i + 1) % count) for i in range(ends)]),
                cells,
                lax.ppermute(head, axis, [((i + 1) % count, i) for i in range(ends)]),
            ],
            axis=dim,
        )
    return cells


def hex_stiffness():
    lame_first = poisson / ((1.0 + poisson) * (1.0 - 2.0 * poisson))
    shear_mod = 1.0 / (2.0 * (1.0 + poisson))
    elastic = np.zeros((6, 6))
    elastic[:3, :3] = lame_first
    for axis_id in range(3):
        elastic[axis_id, axis_id] = lame_first + 2.0 * shear_mod
        elastic[axis_id + 3, axis_id + 3] = shear_mod
    points = [0.5 - 0.5 / np.sqrt(3.0), 0.5 + 0.5 / np.sqrt(3.0)]
    stiffness = np.zeros((24, 24))
    for point_x in points:
        for point_y in points:
            for point_z in points:
                coords = (point_x, point_y, point_z)
                strain = np.zeros((6, 24))
                for corner in range(8):
                    offsets = (corner // 4, corner // 2 % 2, corner % 2)
                    shapes = [
                        coords[axis_id] if offsets[axis_id] == 1 else 1.0 - coords[axis_id]
                        for axis_id in range(3)
                    ]
                    slopes = [1.0 if offsets[axis_id] == 1 else -1.0 for axis_id in range(3)]
                    grad_x = slopes[0] * shapes[1] * shapes[2]
                    grad_y = shapes[0] * slopes[1] * shapes[2]
                    grad_z = shapes[0] * shapes[1] * slopes[2]
                    column = 3 * corner
                    strain[0, column] = grad_x
                    strain[1, column + 1] = grad_y
                    strain[2, column + 2] = grad_z
                    strain[3, column] = grad_y
                    strain[3, column + 1] = grad_x
                    strain[4, column + 1] = grad_z
                    strain[4, column + 2] = grad_y
                    strain[5, column] = grad_z
                    strain[5, column + 2] = grad_x
                stiffness += 0.125 * strain.T @ elastic @ strain
    return stiffness


def blur_weights():
    offsets = np.arange(9) - 4.0
    unscaled = np.exp(-offsets * offsets / (2.0 * blur_sigma * blur_sigma))
    return [float(entry) for entry in unscaled / unscaled.sum()]


def blur_valid(values, axis_id, extent):
    weights = blur_weights()
    summed = weights[0] * lax.slice_in_dim(values, 0, extent, axis=axis_id)
    for tap_index in range(1, 9):
        summed = summed + weights[tap_index] * lax.slice_in_dim(
            values, tap_index, tap_index + extent, axis=axis_id
        )
    return summed


def element_disp(node_field):
    size_x = node_field.shape[1] - 1
    size_y = node_field.shape[2] - 1
    size_z = node_field.shape[3] - 1
    corners = []
    for corner in range(8):
        off_x, off_y, off_z = (corner // 4, corner // 2 % 2, corner % 2)
        corners.append(
            node_field[:, off_x : off_x + size_x, off_y : off_y + size_y, off_z : off_z + size_z]
        )
    return jnp.stack(corners).reshape(24, size_x, size_y, size_z)


def element_forces(node_field, modulus, stiffness):
    local_disp = element_disp(node_field)
    local_force = jnp.einsum("ij,jabc->iabc", stiffness, local_disp, precision=highest) * modulus
    local_force = local_force.reshape((8, 3) + modulus.shape)
    summed = jnp.zeros_like(node_field)
    for corner in range(8):
        off_x, off_y, off_z = (corner // 4, corner // 2 % 2, corner % 2)
        summed = summed + jnp.pad(
            local_force[corner],
            ((0, 0), (off_x, 1 - off_x), (off_y, 1 - off_y), (off_z, 1 - off_z)),
        )
    return summed


def element_energy(node_field, stiffness):
    local_disp = element_disp(node_field)
    local_force = jnp.einsum("ij,jabc->iabc", stiffness, local_disp, precision=highest)
    return jnp.sum(local_disp * local_force, axis=0)


def local_gram(left_field, right_field):
    return jnp.einsum("iabcd,jabcd->ij", left_field, right_field, precision=highest)


def global_gram(left_field, right_field):
    return lax.psum(local_gram(left_field, right_field), ("gx", "gy"))


def mix_cases(field, coeffs):
    return jnp.einsum("kabcd,kj->jabcd", field, coeffs, precision=highest)


def solve_spd(matrix, rhs_matrix):
    factor = jnp.linalg.cholesky(matrix)
    matrix_order = matrix.shape[0]
    forward = []
    for row_index in range(matrix_order):
        partial_sum = rhs_matrix[row_index]
        for col_index in range(row_index):
            partial_sum = partial_sum - factor[row_index, col_index] * forward[col_index]
        forward.append(partial_sum / factor[row_index, row_index])
    backward = [None] * matrix_order
    for row_index in reversed(range(matrix_order)):
        partial_sum = forward[row_index]
        for col_index in range(row_index + 1, matrix_order):
            partial_sum = partial_sum - factor[col_index, row_index] * backward[col_index]
        backward[row_index] = partial_sum / factor[row_index, row_index]
    return jnp.stack(backward)


def pad_upper_z(field):
    return jnp.pad(field, ((0, 0), (0, 0), (0, 0), (0, 0), (0, 1)))


def gather_upper(field):
    from_x = from_behind(field[:, :, :1], "gx", -1)
    widened = jnp.concatenate([field, from_x], axis=2)
    from_y = from_behind(widened[:, :, :, :1], "gy", -1)
    return jnp.concatenate([widened, from_y], axis=3)


def return_lower(forces):
    size_x = forces.shape[2] - 1
    size_y = forces.shape[3] - 1
    to_y = from_behind(forces[:, :, :, size_y:], "gy", 1)
    kept = forces[:, :, :, :size_y]
    kept = jnp.concatenate([kept[:, :, :, :1] + to_y, kept[:, :, :, 1:]], axis=3)
    to_x = from_behind(kept[:, :, size_x:], "gx", 1)
    kept = kept[:, :, :size_x]
    return jnp.concatenate([kept[:, :, :1] + to_x, kept[:, :, 1:]], axis=2)


def on_device(start_disp, bone_mask, density, load_nodes, load_forces):
    stiffness = jnp.asarray(hex_stiffness(), jnp.float32)
    modulus = bone_mask.astype(jnp.float32) * density * density
    case_count = start_disp.shape[0]
    size_x = start_disp.shape[2]
    size_y = start_disp.shape[3]
    size_z = start_disp.shape[4]

    def apply_operator(field):
        node_field = pad_upper_z(gather_upper(field))
        forces = lax.map(
            lambda case_field: element_forces(case_field, modulus, stiffness), node_field
        )
        return return_lower(forces[..., :-1]) + spring * field

    slot_ids = jnp.arange(size_x * size_y, dtype=jnp.int32)
    matches = (load_nodes[0, 0][:, :, None] == slot_ids).astype(jnp.float32)
    top_plane = jnp.einsum("cls,ckl->cks", matches, load_forces[0, 0], precision=highest).reshape(
        case_count, 3, size_x, size_y
    )
    applied = apply_operator(start_disp)
    residual = jnp.concatenate(
        [-applied[..., :-1], (top_plane - applied[..., -1])[..., None]], axis=4
    )
    solution = start_disp
    norm_now = global_gram(residual, residual)
    applied = apply_operator(residual)
    step_alpha = solve_spd(global_gram(residual, applied), norm_now)
    solution = solution + mix_cases(residual, step_alpha)
    node_field = pad_upper_z(gather_upper(solution))
    energy = jnp.sum(
        lax.map(lambda case_field: element_energy(case_field, stiffness), node_field), axis=0
    )
    stimulus = modulus * energy
    smooth = blur_valid(with_halo(stimulus, (("gx", 0),), 4), 0, size_x)
    smooth = blur_valid(with_halo(smooth, (("gy", 1),), 4), 1, size_y)
    smooth = blur_valid(jnp.pad(smooth, ((0, 0), (0, 0), (4, 4))), 2, size_z)
    summed = lax.psum(jnp.sum(smooth), ("gx", "gy"))
    mean_stim = summed / (size_x * size_y * size_z * lax.axis_size("gx") * lax.axis_size("gy"))
    new_density = jnp.minimum(density * (0.5 + 0.5 * smooth / (mean_stim + mean_eps)), density_cap)
    return (solution, new_density)


def solution(mesh):
    return jax.shard_map(
        on_device,
        mesh=mesh,
        in_specs=(
            P(None, None, "gx", "gy", None),
            P("gx", "gy", None),
            P("gx", "gy", None),
            P("gx", "gy", None, None),
            P("gx", "gy", None, None, None),
        ),
        out_specs=(P(None, None, "gx", "gy", None), P("gx", "gy", None)),
        check_vma=False,
    )
```

profile of v0, /device:TPU:1, one launch (start us, length us, event | category | flops | bytes accessed | tf_op | source)
XLA Modules:
  0.0 417.8 jit_solution(12601050354318549686)
XLA Ops:
  0.6 0.9 slice.505
  1.5 1.3 collective-permute-start
  2.8 1.0 constant_dynamic-update-slice_fusion.1
  3.8 4.3 %collective-permute-done = f32[6,3,1,8,128]{4,3,2,1,0:T(8,128)S(1)} collective-permute-done((f32[6,3,1,8,128]{4,3,2,1,0:T(8,128)S(1)}, f32[6,3,1,8,128]{4,3,2,1,0:T(8,128)S(1)}, u32[]{:S(2)}, u32[]{:S(2)}) %collective-permute-start) | collective-permute-done | bytes 73760 | tf_op jit(solution)/shard_map/ppermute | solution.py:18
  8.1 8.5 %collective-permute-start.1 = (f32[6,3,5,1,128]{4,3,2,1,0:T(1,128)S(1)}, f32[6,3,5,1,128]{4,3,2,1,0:T(1,128)S(1)}, u32[]{:S(2)}, u32[]{:S(2)}) collective-permute-start(f32[6,3,5,1,128]{4,3,2,1,0:T(1,128)S(1)} %slice.696), channel_id=1, source_target_pairs={{1,0},{2,1},{3,2},{4,3},{5,4},{6,5},{7,6},{8,7},{9,8},{10,9},{11,1... | collective-permute-start | bytes 138248 | tf_op jit(solution)/shard_map/ppermute | solution.py:18
  18.0 46.3 %while.37 = (s32[]{:T(128)}, f32[6,3,5,9,129]{4,0,3,2,1:T(8,128)S(1)}, f32[6,3,5,9,129]{4,3,2,1,0:T(8,128)S(1)}, f32[4,8,128]{2,1,0:T(8,128)S(1)}, s32[]{:T(128)}, /*index=5*/f32[24,24,1,1]{1,0,3,2:T(8,128)S(1)}, s32[]{:T(128)}) while((s32[]{:T(128)}, f32[6,3,5,9,129]{4,0,3,2,1:T(8,128)S(1)}, ...), condition=%wide.region_1.2_spmd.clone, body=%wide.region_0.1_spmd.sunk.clone.sunk | while | flops 28531760 | bytes 3258905 | solution.py:188
  19.8 5.9 %dynamic_update_slice.27 = f32[6,3,5,9,129]{4,0,3,2,1:T(8,128)S(1)} dynamic-update-slice(f32[6,3,5,9,129]{4,0,3,2,1:T(8,128)S(1)} %get-tuple-element.402, f32[1,3,5,9,129]{4,0,3,2,1:T(1,128)S(1)} %copy.116, s32[]{:T(128)} %get-tuple-element.401, s32[]{:T(128)} %constant.103.clone.1..sunk, s32[]{:T(128)} %constant.103.clone.1..sunk, s32[]{:T(128)} %constant.103.clone.1..sunk, s32[]{:T(128)} %constant.103.clone.1..sunk) | dynamic-update-slice | bytes 139324 | tf_op jit(solution)/shard_map/while/body/jit(dynamic_update_index_in_dim)/dynamic_update_slice | solution.py:188
  27.5 5.9 %dynamic_update_slice.27 = f32[6,3,5,9,129]{4,0,3,2,1:T(8,128)S(1)} dynamic-update-slice(f32[6,3,5,9,129]{4,0,3,2,1:T(8,128)S(1)} %get-tuple-element.402, f32[1,3,5,9,129]{4,0,3,2,1:T(1,128)S(1)} %copy.116, s32[]{:T(128)} %get-tuple-element.401, s32[]{:T(128)} %constant.103.clone.1..sunk, s32[]{:T(128)} %constant.103.clone.1..sunk, s32[]{:T(128)} %constant.103.clone.1..sunk, s32[]{:T(128)} %constant.103.clone.1..sunk) | dynamic-update-slice | bytes 139324 | tf_op jit(solution)/shard_map/while/body/jit(dynamic_update_index_in_dim)/dynamic_update_slice | solution.py:188
  35.2 5.9 %dynamic_update_slice.27 = f32[6,3,5,9,129]{4,0,3,2,1:T(8,128)S(1)} dynamic-update-slice(f32[6,3,5,9,129]{4,0,3,2,1:T(8,128)S(1)} %get-tuple-element.402, f32[1,3,5,9,129]{4,0,3,2,1:T(1,128)S(1)} %copy.116, s32[]{:T(128)} %get-tuple-element.401, s32[]{:T(128)} %constant.103.clone.1..sunk, s32[]{:T(128)} %constant.103.clone.1..sunk, s32[]{:T(128)} %constant.103.clone.1..sunk, s32[]{:T(128)} %constant.103.clone.1..sunk) | dynamic-update-slice | bytes 139324 | tf_op jit(solution)/shard_map/while/body/jit(dynamic_update_index_in_dim)/dynamic_update_slice | solution.py:188
  42.9 5.9 %dynamic_update_slice.27 = f32[6,3,5,9,129]{4,0,3,2,1:T(8,128)S(1)} dynamic-update-slice(f32[6,3,5,9,129]{4,0,3,2,1:T(8,128)S(1)} %get-tuple-element.402, f32[1,3,5,9,129]{4,0,3,2,1:T(1,128)S(1)} %copy.116, s32[]{:T(128)} %get-tuple-element.401, s32[]{:T(128)} %constant.103.clone.1..sunk, s32[]{:T(128)} %constant.103.clone.1..sunk, s32[]{:T(128)} %constant.103.clone.1..sunk, s32[]{:T(128)} %constant.103.clone.1..sunk) | dynamic-update-slice | bytes 139324 | tf_op jit(solution)/shard_map/while/body/jit(dynamic_update_index_in_dim)/dynamic_update_slice | solution.py:188
  50.6 5.9 %dynamic_update_slice.27 = f32[6,3,5,9,129]{4,0,3,2,1:T(8,128)S(1)} dynamic-update-slice(f32[6,3,5,9,129]{4,0,3,2,1:T(8,128)S(1)} %get-tuple-element.402, f32[1,3,5,9,129]{4,0,3,2,1:T(1,128)S(1)} %copy.116, s32[]{:T(128)} %get-tuple-element.401, s32[]{:T(128)} %constant.103.clone.1..sunk, s32[]{:T(128)} %constant.103.clone.1..sunk, s32[]{:T(128)} %constant.103.clone.1..sunk, s32[]{:T(128)} %constant.103.clone.1..sunk) | dynamic-update-slice | bytes 139324 | tf_op jit(solution)/shard_map/while/body/jit(dynamic_update_index_in_dim)/dynamic_update_slice | solution.py:188
  58.3 5.9 %dynamic_update_slice.27 = f32[6,3,5,9,129]{4,0,3,2,1:T(8,128)S(1)} dynamic-update-slice(f32[6,3,5,9,129]{4,0,3,2,1:T(8,128)S(1)} %get-tuple-element.402, f32[1,3,5,9,129]{4,0,3,2,1:T(1,128)S(1)} %copy.116, s32[]{:T(128)} %get-tuple-element.401, s32[]{:T(128)} %constant.103.clone.1..sunk, s32[]{:T(128)} %constant.103.clone.1..sunk, s32[]{:T(128)} %constant.103.clone.1..sunk, s32[]{:T(128)} %constant.103.clone.1..sunk) | dynamic-update-slice | bytes 139324 | tf_op jit(solution)/shard_map/while/body/jit(dynamic_update_index_in_dim)/dynamic_update_slice | solution.py:188
  64.3 1.9 collective-permute-start.2
  66.3 1.2 collective-permute-done.2
  67.6 1.3 collective-permute-start.3
  69.7 1.3 collective-permute-done.3
  71.6 1.3 collective-permute-start.4
  72.9 4.8 %collective-permute-done.4 = f32[6,3,1,8,128]{4,0,3,2,1:T(8,128)S(1)} collective-permute-done((f32[6,3,1,8,128]{4,0,3,2,1:T(8,128)S(1)}, f32[6,3,1,8,128]{4,0,3,2,1:T(8,128)S(1)}, u32[]{:S(2)}, u32[]{:S(2)}) %collective-permute-start.4) | collective-permute-done | bytes 73760 | tf_op jit(solution)/shard_map/ppermute | solution.py:18
  77.8 3.6 collective-permute-start.5
  81.4 3.6 collective-permute-done.5
  85.3 47.1 %while.38 = (s32[]{:T(128)}, f32[6,3,5,9,129]{4,0,3,2,1:T(8,128)S(1)}, f32[6,3,5,9,129]{4,0,3,2,1:T(8,128)S(1)}, f32[4,8,128]{2,1,0:T(8,128)S(1)}, s32[]{:T(128)}, /*index=5*/f32[24,24,1,1]{1,0,3,2:T(8,128)S(1)}, s32[]{:T(128)}) while((s32[]{:T(128)}, f32[6,3,5,9,129]{4,0,3,2,1:T(8,128)S(1)}, ...), condition=%wide.region_4.5_spmd.clone, body=%wide.region_3.4_spmd.sunk.clone.sunk | while | flops 28531760 | bytes 3398225 | solution.py:188
  87.2 5.9 %dynamic_update_slice.28 = f32[6,3,5,9,129]{4,0,3,2,1:T(8,128)S(1)} dynamic-update-slice(f32[6,3,5,9,129]{4,0,3,2,1:T(8,128)S(1)} %get-tuple-element.423, f32[1,3,5,9,129]{4,0,3,2,1:T(1,128)S(1)} %copy.119, s32[]{:T(128)} %get-tuple-element.422, s32[]{:T(128)} %constant.103.clone.1..sunk.1, s32[]{:T(128)} %constant.103.clone.1..sunk.1, s32[]{:T(128)} %constant.103.clone.1..sunk.1, ...) | dynamic-update-slice | bytes 139324 | tf_op jit(solution)/shard_map/while/body/jit(dynamic_update_index_in_dim)/dynamic_update_slice | solution.py:188
  95.1 5.9 %dynamic_update_slice.28 = f32[6,3,5,9,129]{4,0,3,2,1:T(8,128)S(1)} dynamic-update-slice(f32[6,3,5,9,129]{4,0,3,2,1:T(8,128)S(1)} %get-tuple-element.423, f32[1,3,5,9,129]{4,0,3,2,1:T(1,128)S(1)} %copy.119, s32[]{:T(128)} %get-tuple-element.422, s32[]{:T(128)} %constant.103.clone.1..sunk.1, s32[]{:T(128)} %constant.103.clone.1..sunk.1, s32[]{:T(128)} %constant.103.clone.1..sunk.1, ...) | dynamic-update-slice | bytes 139324 | tf_op jit(solution)/shard_map/while/body/jit(dynamic_update_index_in_dim)/dynamic_update_slice | solution.py:188
  102.9 5.9 %dynamic_update_slice.28 = f32[6,3,5,9,129]{4,0,3,2,1:T(8,128)S(1)} dynamic-update-slice(f32[6,3,5,9,129]{4,0,3,2,1:T(8,128)S(1)} %get-tuple-element.423, f32[1,3,5,9,129]{4,0,3,2,1:T(1,128)S(1)} %copy.119, s32[]{:T(128)} %get-tuple-element.422, s32[]{:T(128)} %constant.103.clone.1..sunk.1, s32[]{:T(128)} %constant.103.clone.1..sunk.1, s32[]{:T(128)} %constant.103.clone.1..sunk.1, ...) | dynamic-update-slice | bytes 139324 | tf_op jit(solution)/shard_map/while/body/jit(dynamic_update_index_in_dim)/dynamic_update_slice | solution.py:188
  110.7 5.9 %dynamic_update_slice.28 = f32[6,3,5,9,129]{4,0,3,2,1:T(8,128)S(1)} dynamic-update-slice(f32[6,3,5,9,129]{4,0,3,2,1:T(8,128)S(1)} %get-tuple-element.423, f32[1,3,5,9,129]{4,0,3,2,1:T(1,128)S(1)} %copy.119, s32[]{:T(128)} %get-tuple-element.422, s32[]{:T(128)} %constant.103.clone.1..sunk.1, s32[]{:T(128)} %constant.103.clone.1..sunk.1, s32[]{:T(128)} %constant.103.clone.1..sunk.1, ...) | dynamic-update-slice | bytes 139324 | tf_op jit(solution)/shard_map/while/body/jit(dynamic_update_index_in_dim)/dynamic_update_slice | solution.py:188
  118.6 5.9 %dynamic_update_slice.28 = f32[6,3,5,9,129]{4,0,3,2,1:T(8,128)S(1)} dynamic-update-slice(f32[6,3,5,9,129]{4,0,3,2,1:T(8,128)S(1)} %get-tuple-element.423, f32[1,3,5,9,129]{4,0,3,2,1:T(1,128)S(1)} %copy.119, s32[]{:T(128)} %get-tuple-element.422, s32[]{:T(128)} %constant.103.clone.1..sunk.1, s32[]{:T(128)} %constant.103.clone.1..sunk.1, s32[]{:T(128)} %constant.103.clone.1..sunk.1, ...) | dynamic-update-slice | bytes 139324 | tf_op jit(solution)/shard_map/while/body/jit(dynamic_update_index_in_dim)/dynamic_update_slice | solution.py:188
  126.4 5.9 %dynamic_update_slice.28 = f32[6,3,5,9,129]{4,0,3,2,1:T(8,128)S(1)} dynamic-update-slice(f32[6,3,5,9,129]{4,0,3,2,1:T(8,128)S(1)} %get-tuple-element.423, f32[1,3,5,9,129]{4,0,3,2,1:T(1,128)S(1)} %copy.119, s32[]{:T(128)} %get-tuple-element.422, s32[]{:T(128)} %constant.103.clone.1..sunk.1, s32[]{:T(128)} %constant.103.clone.1..sunk.1, s32[]{:T(128)} %constant.103.clone.1..sunk.1, ...) | dynamic-update-slice | bytes 139324 | tf_op jit(solution)/shard_map/while/body/jit(dynamic_update_index_in_dim)/dynamic_update_slice | solution.py:188
  132.4 1.9 collective-permute-start.6
  134.4 1.2 collective-permute-done.6
  135.6 4.7 %collective-permute-start.7 = (f32[6,3,1,8,128]{4,0,3,2,1:T(8,128)S(1)}, f32[6,3,1,8,128]{4,0,3,2,1:T(8,128)S(1)}, u32[]{:S(2)}, u32[]{:S(2)}) collective-permute-start(f32[6,3,1,8,128]{4,0,3,2,1:T(8,128)S(1)} %pad_maximum_fusion.1), channel_id=1, source_target_pairs={{0,16},{16,32},{32,48},{48,64},{64,80},{80,96},{96,112},{112,128},... | collective-permute-start | bytes 221192 | tf_op jit(solution)/shard_map/ppermute | solution.py:18
  140.3 1.1 convolution_bitcast_fusion.2
  141.4 1.0 collective-permute-done.7
  142.4 1.1 convolution_bitcast_fusion.1
  143.5 108.2 %all-reduce.20 = (f32[6,6]{1,0:T(8,128)S(1)}, f32[6,6]{0,1:T(8,128)S(1)}) all-reduce(f32[6,6]{1,0:T(8,128)S(1)} %convolution_bitcast_fusion.2, f32[6,6]{0,1:T(8,128)S(1)} %convolution_bitcast_fusion.1), channel_id=1, replica_groups=mesh['gx'=32,'gy'=16] {'gx','gy'}, use_global_device_ids=true, to_apply=%region_2.3 | all-reduce | flops 72 | bytes 576 | tf_op jit(solution)/shard_map/psum | solution.py:131
  256.3 9.5 %subtract_divide_fusion.6 = (f32[1,6]{1,0:T(1,128)S(1)}, f32[1,6]{1,0:T(1,128)S(1)}, f32[1,6]{1,0:T(1,128)S(1)}, f32[1,6]{1,0:T(1,128)S(1)}, f32[1,6]{1,0:T(1,128)S(1)}) fusion(f32[6,6]{1,0:T(8,128)S(1)} %get-tuple-element.239, f32[]{:T(128)} %bitcast.19, f32[]{:T(128)} %bitcast.18, f32[]{:T(128)} %bitcast.17, f32[]{:T(128)} %bitcast.16, f32[]{:T(128)} %bitcast.15, ...), kind=kLoop, calls=%fused_computation.219 | loop fusion | flops 150 | bytes 300 | tf_op jit(solution)/shard_map/div | solution.py:146
  265.8 12.6 %subtract_divide_fusion = (f32[1,6]{1,0:T(1,128)S(1)}, f32[1,6]{1,0:T(1,128)S(1)}, f32[1,6]{1,0:T(1,128)S(1)}, f32[1,6]{1,0:T(1,128)S(1)}, f32[1,6]{1,0:T(1,128)S(1)}, /*index=5*/f32[1,6]{1,0:T(1,128)S(1)}) fusion(f32[1,6]{1,0:T(1,128)S(1)} %get-tuple-element.253, f32[]{:T(128)} %bitcast.21, f32[]{:T(128)} %bitcast.16, f32[]{:T(128)} %bitcast.12, ...), kind=kLoop, calls=%fused_computation.213 | loop fusion | flops 276 | bytes 372 | tf_op jit(solution)/shard_map/div | solution.py:152
  279.3 1.3 collective-permute-start.8
  280.6 4.1 collective-permute-done.8
  284.6 3.7 collective-permute-start.9
  288.4 3.8 collective-permute-done.9
  292.3 8.5 %while.39 = (s32[]{:T(128)}, f32[6,4,8,128]{3,2,1,0:T(8,128)S(1)}, f32[6,3,5,9,129]{4,0,3,2,1:T(8,128)S(1)}, s32[]{:T(128)}, f32[24,24,1,1]{1,0,3,2:T(8,128)S(1)}) while((s32[]{:T(128)}, f32[6,4,8,128]{3,2,1,0:T(8,128)S(1)}, f32[6,3,5,9,129]{4,0,3,2,1:T(8,128)S(1)}, s32[]{:T(128)}, f32[24,24,1,1]{1,0,3,2:T(8,128)S(1)}) %tuple.141), condition=%wide.region_10.11_spmd.clone, body=%wide.region_8.10_spmd.sunk.clone.sunk | while | flops 28504064 | bytes 1509813 | solution.py:209
  300.8 1.3 collective-permute-start.10
  302.1 1.3 collective-permute-start.11
  303.5 3.4 collective-permute-done.11
  306.9 3.0 collective-permute-start.12
  309.9 1.9 collective-permute-start.13
  312.6 2.3 collective-permute-done.13
  315.7 100.9 %psum.23 = f32[]{:T(128)} all-reduce(f32[]{:T(128)} %get-tuple-element.241), channel_id=1, replica_groups=mesh['gx'=32,'gy'=16] {'gx','gy'}, use_global_device_ids=true, to_apply=%region_13.14 | all-reduce | flops 1 | bytes 8 | tf_op jit(solution)/shard_map/psum | solution.py:215
  (295 shorter events, 38.6 us)
Async XLA Ops:
  1.5 6.6 %collective-permute-start = (f32[6,3,1,8,128]{4,3,2,1,0:T(8,128)S(1)}, f32[6,3,1,8,128]{4,3,2,1,0:T(8,128)S(1)}, u32[]{:S(2)}, u32[]{:S(2)}) collective-permute-start(f32[6,3,1,8,128]{4,3,2,1,0:T(8,128)S(1)} %slice.505), channel_id=1, source_target_pairs={{16,0},{32,16},{48,32},{64,48},{80,64},{96,80},{112,96},{128,112},... | collective-permute-start | bytes 221192 | tf_op jit(solution)/shard_map/ppermute | solution.py:18
  8.1 9.3 %collective-permute-start.1 = (f32[6,3,5,1,128]{4,3,2,1,0:T(1,128)S(1)}, f32[6,3,5,1,128]{4,3,2,1,0:T(1,128)S(1)}, u32[]{:S(2)}, u32[]{:S(2)}) collective-permute-start(f32[6,3,5,1,128]{4,3,2,1,0:T(1,128)S(1)} %slice.696), channel_id=1, source_target_pairs={{1,0},{2,1},{3,2},{4,3},{5,4},{6,5},{7,6},{8,7},{9,8},{10,9},{11,1... | collective-permute-start | bytes 138248 | tf_op jit(solution)/shard_map/ppermute | solution.py:18
  17.3 0.7 copy-start.1
  18.0 48.2 %copy-start.3 = (s32[1,1,6,32]{3,1,2,0:T(1,128)S(1)}, s32[1,1,6,32]{3,1,2,0:T(1,128)}, u32[]{:S(2)}) copy-start(s32[1,1,6,32]{3,1,2,0:T(1,128)} %param.15) | copy-start | bytes 2308
  64.3 4.6 %copy-start.4 = (f32[1,1,6,3,32]{4,1,3,2,0:T(1,128)S(1)}, f32[1,1,6,3,32]{4,1,3,2,0:T(1,128)}, u32[]{:S(2)}) copy-start(f32[1,1,6,3,32]{4,1,3,2,0:T(1,128)} %param.16) | copy-start | bytes 6916
  64.3 3.2 collective-permute-start.2
  66.3 4.7 %copy-start = (f32[6,3,4,8,128]{4,3,2,1,0:T(8,128)S(1)}, f32[6,3,4,8,128]{4,3,2,1,0:T(8,128)}, u32[]{:S(2)}) copy-start(f32[6,3,4,8,128]{4,3,2,1,0:T(8,128)} %param.12) | copy-start | bytes 884740
  67.6 3.4 collective-permute-start.3
  71.6 6.1 %collective-permute-start.4 = (f32[6,3,1,8,128]{4,0,3,2,1:T(8,128)S(1)}, f32[6,3,1,8,128]{4,0,3,2,1:T(8,128)S(1)}, u32[]{:S(2)}, u32[]{:S(2)}) collective-permute-start(f32[6,3,1,8,128]{4,0,3,2,1:T(8,128)S(1)} %fusion.43), channel_id=1, source_target_pairs={{16,0},{32,16},{48,32},{64,48},{80,64},{96,80},{112,96},{128,112},... | collective-permute-start | bytes 221192 | tf_op jit(solution)/shard_map/ppermute | solution.py:18
  77.8 7.3 %collective-permute-start.5 = (f32[6,3,5,1,128]{4,0,3,2,1:T(8,128)S(1)}, f32[6,3,5,1,128]{4,0,3,2,1:T(8,128)S(1)}, u32[]{:S(2)}, u32[]{:S(2)}) collective-permute-start(f32[6,3,5,1,128]{4,0,3,2,1:T(8,128)S(1)} %pad_maximum_fusion.4), channel_id=1, source_target_pairs={{1,0},{2,1},{3,2},{4,3},{5,4},{6,5},{7,6},{8,7},{9,8},{10,9},{11,1... | collective-permute-start | bytes 138248 | tf_op jit(solution)/shard_map/ppermute | solution.py:18
  132.4 3.2 collective-permute-start.6
  135.6 6.8 %collective-permute-start.7 = (f32[6,3,1,8,128]{4,0,3,2,1:T(8,128)S(1)}, f32[6,3,1,8,128]{4,0,3,2,1:T(8,128)S(1)}, u32[]{:S(2)}, u32[]{:S(2)}) collective-permute-start(f32[6,3,1,8,128]{4,0,3,2,1:T(8,128)S(1)} %pad_maximum_fusion.1), channel_id=1, source_target_pairs={{0,16},{16,32},{32,48},{48,64},{64,80},{80,96},{96,112},{112,128},... | collective-permute-start | bytes 221192 | tf_op jit(solution)/shard_map/ppermute | solution.py:18
  279.3 5.4 %collective-permute-start.8 = (f32[6,3,1,8,128]{4,0,3,2,1:T(8,128)S(1)}, f32[6,3,1,8,128]{4,0,3,2,1:T(8,128)S(1)}, u32[]{:S(2)}, u32[]{:S(2)}) collective-permute-start(f32[6,3,1,8,128]{4,0,3,2,1:T(8,128)S(1)} %slice.701), channel_id=1, source_target_pairs={{16,0},{32,16},{48,32},{64,48},{80,64},{96,80},{112,96},{128,112},... | collective-permute-start | bytes 221192 | tf_op jit(solution)/shard_map/ppermute | solution.py:18
  284.6 7.5 %collective-permute-start.9 = (f32[6,3,5,1,128]{4,0,3,2,1:T(8,128)S(1)}, f32[6,3,5,1,128]{4,0,3,2,1:T(8,128)S(1)}, u32[]{:S(2)}, u32[]{:S(2)}) collective-permute-start(f32[6,3,5,1,128]{4,0,3,2,1:T(8,128)S(1)} %pad_maximum_fusion.3), channel_id=1, source_target_pairs={{1,0},{2,1},{3,2},{4,3},{5,4},{6,5},{7,6},{8,7},{9,8},{10,9},{11,1... | collective-permute-start | bytes 138248 | tf_op jit(solution)/shard_map/ppermute | solution.py:18
  292.3 124.9 %copy-start.2 = (f32[4,8,128]{2,1,0:T(8,128)S(1)}, f32[4,8,128]{2,1,0:T(8,128)}, u32[]{:S(2)}) copy-start(f32[4,8,128]{2,1,0:T(8,128)} %param.14) | copy-start | bytes 49156
  300.8 2.6 collective-permute-start.10
  302.1 4.7 %collective-permute-start.11 = (f32[4,8,128]{2,1,0:T(8,128)S(1)}, f32[4,8,128]{2,1,0:T(8,128)S(1)}, u32[]{:S(2)}, u32[]{:S(2)}) collective-permute-start(f32[4,8,128]{2,1,0:T(8,128)S(1)} %mul.463), channel_id=1, source_target_pairs={{16,0},{32,16},{48,32},{64,48},{80,64},{96,80},{112,96},{128,112},... | collective-permute-start | bytes 49160 | tf_op jit(solution)/shard_map/ppermute | solution.py:31
  306.9 5.7 %collective-permute-start.12 = (f32[4,4,128]{2,1,0:T(4,128)S(1)}, f32[4,4,128]{2,1,0:T(4,128)S(1)}, u32[]{:S(2)}, u32[]{:S(2)}) collective-permute-start(f32[4,4,128]{2,1,0:T(4,128)S(1)} %get-tuple-element.270), channel_id=1, source_target_pairs={{0,1},{1,2},{2,3},{3,4},{4,5},{5,6},{6,7},{7,8},{8,9},{9,10},{10,1... | collective-permute-start | bytes 24584 | tf_op jit(solution)/shard_map/ppermute | solution.py:29
  309.9 5.0 %collective-permute-start.13 = (f32[4,4,128]{2,1,0:T(4,128)S(1)}, f32[4,4,128]{2,1,0:T(4,128)S(1)}, u32[]{:S(2)}, u32[]{:S(2)}) collective-permute-start(f32[4,4,128]{2,1,0:T(4,128)S(1)} %get-tuple-element.271), channel_id=1, source_target_pairs={{1,0},{2,1},{3,2},{4,3},{5,4},{6,5},{7,6},{8,7},{9,8},{10,9},{11,1... | collective-permute-start | bytes 24584 | tf_op jit(solution)/shard_map/ppermute | solution.py:31
where the time goes:
time: 419 us; the launch traced here: 418 us
  blocking collectives  209 us (50%)
  local copies, waits for them, and re-layouts  88.3 us (21%)
  starting transfers between devices  37.1 us (9%)
  other arithmetic  31.3 us (7%)
  waiting for transfers between devices  31.1 us (7%)
  matrix products  16.5 us (4%)
    psum x1, blocking collectives, global_gram(): return lax.psum(local_gram(left_field, right_field), ('gx', 'gy'))  108 us
    psum x1, blocking collectives, on_device(): summed = lax.psum(jnp.sum(smooth), ('gx', 'gy'))  101 us
    dynamic_update_slice x24, local copies, waits for them, and re-layouts, apply_operator(): lax.map(lambda case_field: element_forces(case_field, modulus, stiffness)...  73.1 us
    ppermute x10, starting transfers between devices, from_behind(): return lax.ppermute(block, axis, route)  29.5 us
    ppermute x10, waiting for transfers between devices, from_behind(): return lax.ppermute(block, axis, route)  25.4 us
    div x1, other arithmetic, solve_spd(): backward[row_index] = partial_sum / factor[row_index, row_index]  12.6 us
    div x1, other arithmetic, solve_spd(): forward.append(partial_sum / factor[row_index, row_index])  9.49 us
  transfers between devices with their start and end apart: 14, of which 12 were waited for; matrix products, arithmetic and copies ran while one was open for 1% of the time, Pallas kernels for 0%

commit v1 on v0

--- a/solution.py
+++ b/solution.py
@@ -128,7 +128,8 @@
 
 
 def global_gram(left_field, right_field):
-    return lax.psum(local_gram(left_field, right_field), ("gx", "gy"))
+    _lead_ways = lambda here_x: lax.psum(lax.psum(here_x, "gx"), "gy")
+    return _lead_ways(local_gram(left_field, right_field))
 
 
 def mix_cases(field, coeffs):

time: 419 us -> 412 us (0.983)
  blocking collectives: 209 us -> 203 us
    psum x1 -> x2, blocking collectives: 108 us -> 104 us  [global_gram(): _lead_ways = lambda here_x: lax.psum(lax.psum(here_x, 'gx'), 'gy')]
where the time goes in v1:
time: 412 us; the launch traced here: 410 us
  blocking collectives  203 us (49%)
  local copies, waits for them, and re-layouts  88.2 us (21%)
  starting transfers between devices  36.4 us (9%)
  other arithmetic  31.1 us (8%)
  waiting for transfers between devices  30.5 us (7%)
  matrix products  16.5 us (4%)
    psum x2, blocking collectives, global_gram(): _lead_ways = lambda here_x: lax.psum(lax.psum(here_x, 'gx'), 'gy')  104 us
    psum x1, blocking collectives, on_device(): summed = lax.psum(jnp.sum(smooth), ('gx', 'gy'))  98.6 us
    dynamic_update_slice x24, local copies, waits for them, and re-layouts, apply_operator(): lax.map(lambda case_field: element_forces(case_field, modulus, stiffness)...  73.1 us
    ppermute x10, starting transfers between devices, from_behind(): return lax.ppermute(block, axis, route)  28.7 us
    ppermute x10, waiting for transfers between devices, from_behind(): return lax.ppermute(block, axis, route)  25 us
    div x1, other arithmetic, solve_spd(): backward[row_index] = partial_sum / factor[row_index, row_index]  12.6 us
    div x1, other arithmetic, solve_spd(): forward.append(partial_sum / factor[row_index, row_index])  9.36 us
    dot_general x12, matrix products, element_forces(): jnp.einsum('ij,jabc->iabc', stiffness, local_disp, precision=highest)  8.27 us
  transfers between devices with their start and end apart: 14, of which 12 were waited for; matrix products, arithmetic and copies ran while one was open for 1% of the time, Pallas kernels for 0%

profile of v1, /device:TPU:1, one launch (start us, length us, event | category | flops | bytes accessed | tf_op | source)
XLA Modules:
  0.0 409.9 jit_solution(4840381124514323695)
XLA Ops:
  1.5 1.3 collective-permute-start
  2.8 1.0 constant_dynamic-update-slice_fusion.1
  3.8 4.3 %collective-permute-done = f32[6,3,1,8,128]{4,3,2,1,0:T(8,128)S(1)} collective-permute-done((f32[6,3,1,8,128]{4,3,2,1,0:T(8,128)S(1)}, f32[6,3,1,8,128]{4,3,2,1,0:T(8,128)S(1)}, u32[]{:S(2)}, u32[]{:S(2)}) %collective-permute-start) | collective-permute-done | bytes 73760 | tf_op jit(solution)/shard_map/ppermute | solution.py:18
  8.1 8.5 %collective-permute-start.1 = (f32[6,3,5,1,128]{4,3,2,1,0:T(1,128)S(1)}, f32[6,3,5,1,128]{4,3,2,1,0:T(1,128)S(1)}, u32[]{:S(2)}, u32[]{:S(2)}) collective-permute-start(f32[6,3,5,1,128]{4,3,2,1,0:T(1,128)S(1)} %slice.696), channel_id=1, source_target_pairs={{1,0},{2,1},{3,2},{4,3},{5,4},{6,5},{7,6},{8,7},{9,8},{10,9},{11,1... | collective-permute-start | bytes 138248 | tf_op jit(solution)/shard_map/ppermute | solution.py:18
  18.0 46.3 %while.37 = (s32[]{:T(128)}, f32[6,3,5,9,129]{4,0,3,2,1:T(8,128)S(1)}, f32[6,3,5,9,129]{4,3,2,1,0:T(8,128)S(1)}, f32[4,8,128]{2,1,0:T(8,128)S(1)}, s32[]{:T(128)}, /*index=5*/f32[24,24,1,1]{1,0,3,2:T(8,128)S(1)}, s32[]{:T(128)}) while((s32[]{:T(128)}, f32[6,3,5,9,129]{4,0,3,2,1:T(8,128)S(1)}, ...), condition=%wide.region_1.2_spmd.clone, body=%wide.region_0.1_spmd.sunk.clone.sunk | while | flops 28531760 | bytes 3258905 | solution.py:189
  19.8 5.9 %dynamic_update_slice.27 = f32[6,3,5,9,129]{4,0,3,2,1:T(8,128)S(1)} dynamic-update-slice(f32[6,3,5,9,129]{4,0,3,2,1:T(8,128)S(1)} %get-tuple-element.404, f32[1,3,5,9,129]{4,0,3,2,1:T(1,128)S(1)} %copy.116, s32[]{:T(128)} %get-tuple-element.403, s32[]{:T(128)} %constant.103.clone.1..sunk, s32[]{:T(128)} %constant.103.clone.1..sunk, s32[]{:T(128)} %constant.103.clone.1..sunk, s32[]{:T(128)} %constant.103.clone.1..sunk) | dynamic-update-slice | bytes 139324 | tf_op jit(solution)/shard_map/while/body/jit(dynamic_update_index_in_dim)/dynamic_update_slice | solution.py:189
  27.5 5.9 %dynamic_update_slice.27 = f32[6,3,5,9,129]{4,0,3,2,1:T(8,128)S(1)} dynamic-update-slice(f32[6,3,5,9,129]{4,0,3,2,1:T(8,128)S(1)} %get-tuple-element.404, f32[1,3,5,9,129]{4,0,3,2,1:T(1,128)S(1)} %copy.116, s32[]{:T(128)} %get-tuple-element.403, s32[]{:T(128)} %constant.103.clone.1..sunk, s32[]{:T(128)} %constant.103.clone.1..sunk, s32[]{:T(128)} %constant.103.clone.1..sunk, s32[]{:T(128)} %constant.103.clone.1..sunk) | dynamic-update-slice | bytes 139324 | tf_op jit(solution)/shard_map/while/body/jit(dynamic_update_index_in_dim)/dynamic_update_slice | solution.py:189
  35.2 5.9 %dynamic_update_slice.27 = f32[6,3,5,9,129]{4,0,3,2,1:T(8,128)S(1)} dynamic-update-slice(f32[6,3,5,9,129]{4,0,3,2,1:T(8,128)S(1)} %get-tuple-element.404, f32[1,3,5,9,129]{4,0,3,2,1:T(1,128)S(1)} %copy.116, s32[]{:T(128)} %get-tuple-element.403, s32[]{:T(128)} %constant.103.clone.1..sunk, s32[]{:T(128)} %constant.103.clone.1..sunk, s32[]{:T(128)} %constant.103.clone.1..sunk, s32[]{:T(128)} %constant.103.clone.1..sunk) | dynamic-update-slice | bytes 139324 | tf_op jit(solution)/shard_map/while/body/jit(dynamic_update_index_in_dim)/dynamic_update_slice | solution.py:189
  42.9 5.9 %dynamic_update_slice.27 = f32[6,3,5,9,129]{4,0,3,2,1:T(8,128)S(1)} dynamic-update-slice(f32[6,3,5,9,129]{4,0,3,2,1:T(8,128)S(1)} %get-tuple-element.404, f32[1,3,5,9,129]{4,0,3,2,1:T(1,128)S(1)} %copy.116, s32[]{:T(128)} %get-tuple-element.403, s32[]{:T(128)} %constant.103.clone.1..sunk, s32[]{:T(128)} %constant.103.clone.1..sunk, s32[]{:T(128)} %constant.103.clone.1..sunk, s32[]{:T(128)} %constant.103.clone.1..sunk) | dynamic-update-slice | bytes 139324 | tf_op jit(solution)/shard_map/while/body/jit(dynamic_update_index_in_dim)/dynamic_update_slice | solution.py:189
  50.6 5.9 %dynamic_update_slice.27 = f32[6,3,5,9,129]{4,0,3,2,1:T(8,128)S(1)} dynamic-update-slice(f32[6,3,5,9,129]{4,0,3,2,1:T(8,128)S(1)} %get-tuple-element.404, f32[1,3,5,9,129]{4,0,3,2,1:T(1,128)S(1)} %copy.116, s32[]{:T(128)} %get-tuple-element.403, s32[]{:T(128)} %constant.103.clone.1..sunk, s32[]{:T(128)} %constant.103.clone.1..sunk, s32[]{:T(128)} %constant.103.clone.1..sunk, s32[]{:T(128)} %constant.103.clone.1..sunk) | dynamic-update-slice | bytes 139324 | tf_op jit(solution)/shard_map/while/body/jit(dynamic_update_index_in_dim)/dynamic_update_slice | solution.py:189
  58.3 5.9 %dynamic_update_slice.27 = f32[6,3,5,9,129]{4,0,3,2,1:T(8,128)S(1)} dynamic-update-slice(f32[6,3,5,9,129]{4,0,3,2,1:T(8,128)S(1)} %get-tuple-element.404, f32[1,3,5,9,129]{4,0,3,2,1:T(1,128)S(1)} %copy.116, s32[]{:T(128)} %get-tuple-element.403, s32[]{:T(128)} %constant.103.clone.1..sunk, s32[]{:T(128)} %constant.103.clone.1..sunk, s32[]{:T(128)} %constant.103.clone.1..sunk, s32[]{:T(128)} %constant.103.clone.1..sunk) | dynamic-update-slice | bytes 139324 | tf_op jit(solution)/shard_map/while/body/jit(dynamic_update_index_in_dim)/dynamic_update_slice | solution.py:189
  64.3 1.9 collective-permute-start.2
  66.3 1.2 collective-permute-done.2
  67.6 1.3 collective-permute-start.3
  69.7 1.3 collective-permute-done.3
  71.6 1.3 collective-permute-start.4
  72.9 4.8 %collective-permute-done.4 = f32[6,3,1,8,128]{4,0,3,2,1:T(8,128)S(1)} collective-permute-done((f32[6,3,1,8,128]{4,0,3,2,1:T(8,128)S(1)}, f32[6,3,1,8,128]{4,0,3,2,1:T(8,128)S(1)}, u32[]{:S(2)}, u32[]{:S(2)}) %collective-permute-start.4) | collective-permute-done | bytes 73760 | tf_op jit(solution)/shard_map/ppermute | solution.py:18
  77.8 3.6 collective-permute-start.5
  81.4 3.6 collective-permute-done.5
  85.3 47.1 %while.38 = (s32[]{:T(128)}, f32[6,3,5,9,129]{4,0,3,2,1:T(8,128)S(1)}, f32[6,3,5,9,129]{4,0,3,2,1:T(8,128)S(1)}, f32[4,8,128]{2,1,0:T(8,128)S(1)}, s32[]{:T(128)}, /*index=5*/f32[24,24,1,1]{1,0,3,2:T(8,128)S(1)}, s32[]{:T(128)}) while((s32[]{:T(128)}, f32[6,3,5,9,129]{4,0,3,2,1:T(8,128)S(1)}, ...), condition=%wide.region_5.6_spmd.clone, body=%wide.region_4.5_spmd.sunk.clone.sunk | while | flops 28531760 | bytes 3398225 | solution.py:189
  87.2 5.9 %dynamic_update_slice.28 = f32[6,3,5,9,129]{4,0,3,2,1:T(8,128)S(1)} dynamic-update-slice(f32[6,3,5,9,129]{4,0,3,2,1:T(8,128)S(1)} %get-tuple-element.425, f32[1,3,5,9,129]{4,0,3,2,1:T(1,128)S(1)} %copy.119, s32[]{:T(128)} %get-tuple-element.424, s32[]{:T(128)} %constant.103.clone.1..sunk.1, s32[]{:T(128)} %constant.103.clone.1..sunk.1, s32[]{:T(128)} %constant.103.clone.1..sunk.1, ...) | dynamic-update-slice | bytes 139324 | tf_op jit(solution)/shard_map/while/body/jit(dynamic_update_index_in_dim)/dynamic_update_slice | solution.py:189
  95.1 5.9 %dynamic_update_slice.28 = f32[6,3,5,9,129]{4,0,3,2,1:T(8,128)S(1)} dynamic-update-slice(f32[6,3,5,9,129]{4,0,3,2,1:T(8,128)S(1)} %get-tuple-element.425, f32[1,3,5,9,129]{4,0,3,2,1:T(1,128)S(1)} %copy.119, s32[]{:T(128)} %get-tuple-element.424, s32[]{:T(128)} %constant.103.clone.1..sunk.1, s32[]{:T(128)} %constant.103.clone.1..sunk.1, s32[]{:T(128)} %constant.103.clone.1..sunk.1, ...) | dynamic-update-slice | bytes 139324 | tf_op jit(solution)/shard_map/while/body/jit(dynamic_update_index_in_dim)/dynamic_update_slice | solution.py:189
  102.9 5.9 %dynamic_update_slice.28 = f32[6,3,5,9,129]{4,0,3,2,1:T(8,128)S(1)} dynamic-update-slice(f32[6,3,5,9,129]{4,0,3,2,1:T(8,128)S(1)} %get-tuple-element.425, f32[1,3,5,9,129]{4,0,3,2,1:T(1,128)S(1)} %copy.119, s32[]{:T(128)} %get-tuple-element.424, s32[]{:T(128)} %constant.103.clone.1..sunk.1, s32[]{:T(128)} %constant.103.clone.1..sunk.1, s32[]{:T(128)} %constant.103.clone.1..sunk.1, ...) | dynamic-update-slice | bytes 139324 | tf_op jit(solution)/shard_map/while/body/jit(dynamic_update_index_in_dim)/dynamic_update_slice | solution.py:189
  110.7 5.9 %dynamic_update_slice.28 = f32[6,3,5,9,129]{4,0,3,2,1:T(8,128)S(1)} dynamic-update-slice(f32[6,3,5,9,129]{4,0,3,2,1:T(8,128)S(1)} %get-tuple-element.425, f32[1,3,5,9,129]{4,0,3,2,1:T(1,128)S(1)} %copy.119, s32[]{:T(128)} %get-tuple-element.424, s32[]{:T(128)} %constant.103.clone.1..sunk.1, s32[]{:T(128)} %constant.103.clone.1..sunk.1, s32[]{:T(128)} %constant.103.clone.1..sunk.1, ...) | dynamic-update-slice | bytes 139324 | tf_op jit(solution)/shard_map/while/body/jit(dynamic_update_index_in_dim)/dynamic_update_slice | solution.py:189
  118.6 5.9 %dynamic_update_slice.28 = f32[6,3,5,9,129]{4,0,3,2,1:T(8,128)S(1)} dynamic-update-slice(f32[6,3,5,9,129]{4,0,3,2,1:T(8,128)S(1)} %get-tuple-element.425, f32[1,3,5,9,129]{4,0,3,2,1:T(1,128)S(1)} %copy.119, s32[]{:T(128)} %get-tuple-element.424, s32[]{:T(128)} %constant.103.clone.1..sunk.1, s32[]{:T(128)} %constant.103.clone.1..sunk.1, s32[]{:T(128)} %constant.103.clone.1..sunk.1, ...) | dynamic-update-slice | bytes 139324 | tf_op jit(solution)/shard_map/while/body/jit(dynamic_update_index_in_dim)/dynamic_update_slice | solution.py:189
  126.4 5.9 %dynamic_update_slice.28 = f32[6,3,5,9,129]{4,0,3,2,1:T(8,128)S(1)} dynamic-update-slice(f32[6,3,5,9,129]{4,0,3,2,1:T(8,128)S(1)} %get-tuple-element.425, f32[1,3,5,9,129]{4,0,3,2,1:T(1,128)S(1)} %copy.119, s32[]{:T(128)} %get-tuple-element.424, s32[]{:T(128)} %constant.103.clone.1..sunk.1, s32[]{:T(128)} %constant.103.clone.1..sunk.1, s32[]{:T(128)} %constant.103.clone.1..sunk.1, ...) | dynamic-update-slice | bytes 139324 | tf_op jit(solution)/shard_map/while/body/jit(dynamic_update_index_in_dim)/dynamic_update_slice | solution.py:189
  132.4 1.9 collective-permute-start.6
  134.4 1.2 collective-permute-done.6
  135.6 4.7 %collective-permute-start.7 = (f32[6,3,1,8,128]{4,0,3,2,1:T(8,128)S(1)}, f32[6,3,1,8,128]{4,0,3,2,1:T(8,128)S(1)}, u32[]{:S(2)}, u32[]{:S(2)}) collective-permute-start(f32[6,3,1,8,128]{4,0,3,2,1:T(8,128)S(1)} %pad_maximum_fusion.1), channel_id=1, source_target_pairs={{0,16},{16,32},{32,48},{48,64},{64,80},{80,96},{96,112},{112,128},... | collective-permute-start | bytes 221192 | tf_op jit(solution)/shard_map/ppermute | solution.py:18
  140.3 1.1 convolution_bitcast_fusion.2
  141.4 1.0 collective-permute-done.7
  142.4 1.1 convolution_bitcast_fusion.1
  143.5 64.9 %all-reduce.20 = (f32[6,6]{1,0:T(8,128)S(1)}, f32[6,6]{0,1:T(8,128)S(1)}) all-reduce(f32[6,6]{1,0:T(8,128)S(1)} %convolution_bitcast_fusion.2, f32[6,6]{0,1:T(8,128)S(1)} %convolution_bitcast_fusion.1), channel_id=1, replica_groups=mesh['gx'=32,'gy'=16] {'gx'}, use_global_device_ids=true, to_apply=%region_2.3 | all-reduce | flops 72 | bytes 576 | tf_op jit(solution)/shard_map/psum | solution.py:131
  208.4 39.2 %all-reduce.21 = (f32[6,6]{1,0:T(8,128)S(1)}, f32[6,6]{0,1:T(8,128)S(1)}) all-reduce(f32[6,6]{1,0:T(8,128)S(1)} %get-tuple-element.239, f32[6,6]{0,1:T(8,128)S(1)} %get-tuple-element.240), channel_id=1, replica_groups=mesh['gx'=32,'gy'=16] {'gy'}, use_global_device_ids=true, to_apply=%region_3.4 | all-reduce | flops 72 | bytes 576 | tf_op jit(solution)/shard_map/psum | solution.py:131
  252.2 9.4 %subtract_divide_fusion.6 = (f32[1,6]{1,0:T(1,128)S(1)}, f32[1,6]{1,0:T(1,128)S(1)}, f32[1,6]{1,0:T(1,128)S(1)}, f32[1,6]{1,0:T(1,128)S(1)}, f32[1,6]{1,0:T(1,128)S(1)}) fusion(f32[6,6]{1,0:T(8,128)S(1)} %get-tuple-element.241, f32[]{:T(128)} %bitcast.19, f32[]{:T(128)} %bitcast.18, f32[]{:T(128)} %bitcast.17, f32[]{:T(128)} %bitcast.16, f32[]{:T(128)} %bitcast.15, ...), kind=kLoop, calls=%fused_computation.219 | loop fusion | flops 150 | bytes 300 | tf_op jit(solution)/shard_map/div | solution.py:147
  261.6 12.6 %subtract_divide_fusion = (f32[1,6]{1,0:T(1,128)S(1)}, f32[1,6]{1,0:T(1,128)S(1)}, f32[1,6]{1,0:T(1,128)S(1)}, f32[1,6]{1,0:T(1,128)S(1)}, f32[1,6]{1,0:T(1,128)S(1)}, /*index=5*/f32[1,6]{1,0:T(1,128)S(1)}) fusion(f32[1,6]{1,0:T(1,128)S(1)} %get-tuple-element.255, f32[]{:T(128)} %bitcast.21, f32[]{:T(128)} %bitcast.16, f32[]{:T(128)} %bitcast.12, ...), kind=kLoop, calls=%fused_computation.213 | loop fusion | flops 276 | bytes 372 | tf_op jit(solution)/shard_map/div | solution.py:153
  275.0 1.3 collective-permute-start.8
  276.3 4.8 %collective-permute-done.8 = f32[6,3,1,8,128]{4,0,3,2,1:T(8,128)S(1)} collective-permute-done((f32[6,3,1,8,128]{4,0,3,2,1:T(8,128)S(1)}, f32[6,3,1,8,128]{4,0,3,2,1:T(8,128)S(1)}, u32[]{:S(2)}, u32[]{:S(2)}) %collective-permute-start.8) | collective-permute-done | bytes 73760 | tf_op jit(solution)/shard_map/ppermute | solution.py:18
  281.1 2.9 collective-permute-start.9
  284.0 2.7 collective-permute-done.9
  286.8 8.5 %while.39 = (s32[]{:T(128)}, f32[6,4,8,128]{3,2,1,0:T(8,128)S(1)}, f32[6,3,5,9,129]{4,0,3,2,1:T(8,128)S(1)}, s32[]{:T(128)}, f32[24,24,1,1]{1,0,3,2:T(8,128)S(1)}) while((s32[]{:T(128)}, f32[6,4,8,128]{3,2,1,0:T(8,128)S(1)}, f32[6,3,5,9,129]{4,0,3,2,1:T(8,128)S(1)}, s32[]{:T(128)}, f32[24,24,1,1]{1,0,3,2:T(8,128)S(1)}) %tuple.141), condition=%wide.region_12.13_spmd.clone, body=%wide.region_10.12_spmd.sunk.clone.sunk | while | flops 28504064 | bytes 1509813 | solution.py:210
  295.4 1.3 collective-permute-start.10
  296.7 1.3 collective-permute-start.11
  298.0 3.2 collective-permute-done.11
  301.2 3.2 collective-permute-start.12
  304.4 1.9 collective-permute-start.13
  307.1 2.3 collective-permute-done.13
  310.1 98.6 %psum.39 = f32[]{:T(128)} all-reduce(f32[]{:T(128)} %get-tuple-element.243), channel_id=1, replica_groups=mesh['gx'=32,'gy'=16] {'gx','gy'}, use_global_device_ids=true, to_apply=%region_15.16 | all-reduce | flops 1 | bytes 8 | tf_op jit(solution)/shard_map/psum | solution.py:216
  (296 shorter events, 39.5 us)
Async XLA Ops:
  1.5 6.6 %collective-permute-start = (f32[6,3,1,8,128]{4,3,2,1,0:T(8,128)S(1)}, f32[6,3,1,8,128]{4,3,2,1,0:T(8,128)S(1)}, u32[]{:S(2)}, u32[]{:S(2)}) collective-permute-start(f32[6,3,1,8,128]{4,3,2,1,0:T(8,128)S(1)} %slice.505), channel_id=1, source_target_pairs={{16,0},{32,16},{48,32},{64,48},{80,64},{96,80},{112,96},{128,112},... | collective-permute-start | bytes 221192 | tf_op jit(solution)/shard_map/ppermute | solution.py:18
  8.1 9.3 %collective-permute-start.1 = (f32[6,3,5,1,128]{4,3,2,1,0:T(1,128)S(1)}, f32[6,3,5,1,128]{4,3,2,1,0:T(1,128)S(1)}, u32[]{:S(2)}, u32[]{:S(2)}) collective-permute-start(f32[6,3,5,1,128]{4,3,2,1,0:T(1,128)S(1)} %slice.696), channel_id=1, source_target_pairs={{1,0},{2,1},{3,2},{4,3},{5,4},{6,5},{7,6},{8,7},{9,8},{10,9},{11,1... | collective-permute-start | bytes 138248 | tf_op jit(solution)/shard_map/ppermute | solution.py:18
  17.3 0.7 copy-start.1
  18.0 48.2 %copy-start.3 = (s32[1,1,6,32]{3,1,2,0:T(1,128)S(1)}, s32[1,1,6,32]{3,1,2,0:T(1,128)}, u32[]{:S(2)}) copy-start(s32[1,1,6,32]{3,1,2,0:T(1,128)} %param.15) | copy-start | bytes 2308
  64.3 4.6 %copy-start.4 = (f32[1,1,6,3,32]{4,1,3,2,0:T(1,128)S(1)}, f32[1,1,6,3,32]{4,1,3,2,0:T(1,128)}, u32[]{:S(2)}) copy-start(f32[1,1,6,3,32]{4,1,3,2,0:T(1,128)} %param.16) | copy-start | bytes 6916
  64.3 3.2 collective-permute-start.2
  66.3 4.7 %copy-start = (f32[6,3,4,8,128]{4,3,2,1,0:T(8,128)S(1)}, f32[6,3,4,8,128]{4,3,2,1,0:T(8,128)}, u32[]{:S(2)}) copy-start(f32[6,3,4,8,128]{4,3,2,1,0:T(8,128)} %param.12) | copy-start | bytes 884740
  67.6 3.4 collective-permute-start.3
  71.6 6.1 %collective-permute-start.4 = (f32[6,3,1,8,128]{4,0,3,2,1:T(8,128)S(1)}, f32[6,3,1,8,128]{4,0,3,2,1:T(8,128)S(1)}, u32[]{:S(2)}, u32[]{:S(2)}) collective-permute-start(f32[6,3,1,8,128]{4,0,3,2,1:T(8,128)S(1)} %fusion.43), channel_id=1, source_target_pairs={{16,0},{32,16},{48,32},{64,48},{80,64},{96,80},{112,96},{128,112},... | collective-permute-start | bytes 221192 | tf_op jit(solution)/shard_map/ppermute | solution.py:18
  77.8 7.3 %collective-permute-start.5 = (f32[6,3,5,1,128]{4,0,3,2,1:T(8,128)S(1)}, f32[6,3,5,1,128]{4,0,3,2,1:T(8,128)S(1)}, u32[]{:S(2)}, u32[]{:S(2)}) collective-permute-start(f32[6,3,5,1,128]{4,0,3,2,1:T(8,128)S(1)} %pad_maximum_fusion.4), channel_id=1, source_target_pairs={{1,0},{2,1},{3,2},{4,3},{5,4},{6,5},{7,6},{8,7},{9,8},{10,9},{11,1... | collective-permute-start | bytes 138248 | tf_op jit(solution)/shard_map/ppermute | solution.py:18
  132.4 3.2 collective-permute-start.6
  135.6 6.8 %collective-permute-start.7 = (f32[6,3,1,8,128]{4,0,3,2,1:T(8,128)S(1)}, f32[6,3,1,8,128]{4,0,3,2,1:T(8,128)S(1)}, u32[]{:S(2)}, u32[]{:S(2)}) collective-permute-start(f32[6,3,1,8,128]{4,0,3,2,1:T(8,128)S(1)} %pad_maximum_fusion.1), channel_id=1, source_target_pairs={{0,16},{16,32},{32,48},{48,64},{64,80},{80,96},{96,112},{112,128},... | collective-permute-start | bytes 221192 | tf_op jit(solution)/shard_map/ppermute | solution.py:18
  275.0 6.1 %collective-permute-start.8 = (f32[6,3,1,8,128]{4,0,3,2,1:T(8,128)S(1)}, f32[6,3,1,8,128]{4,0,3,2,1:T(8,128)S(1)}, u32[]{:S(2)}, u32[]{:S(2)}) collective-permute-start(f32[6,3,1,8,128]{4,0,3,2,1:T(8,128)S(1)} %slice.701), channel_id=1, source_target_pairs={{16,0},{32,16},{48,32},{64,48},{80,64},{96,80},{112,96},{128,112},... | collective-permute-start | bytes 221192 | tf_op jit(solution)/shard_map/ppermute | solution.py:18
  281.1 5.5 %collective-permute-start.9 = (f32[6,3,5,1,128]{4,0,3,2,1:T(8,128)S(1)}, f32[6,3,5,1,128]{4,0,3,2,1:T(8,128)S(1)}, u32[]{:S(2)}, u32[]{:S(2)}) collective-permute-start(f32[6,3,5,1,128]{4,0,3,2,1:T(8,128)S(1)} %pad_maximum_fusion.3), channel_id=1, source_target_pairs={{1,0},{2,1},{3,2},{4,3},{5,4},{6,5},{7,6},{8,7},{9,8},{10,9},{11,1... | collective-permute-start | bytes 138248 | tf_op jit(solution)/shard_map/ppermute | solution.py:18
  286.8 122.5 %copy-start.2 = (f32[4,8,128]{2,1,0:T(8,128)S(1)}, f32[4,8,128]{2,1,0:T(8,128)}, u32[]{:S(2)}) copy-start(f32[4,8,128]{2,1,0:T(8,128)} %param.14) | copy-start | bytes 49156
  295.4 2.6 collective-permute-start.10
  296.7 4.5 %collective-permute-start.11 = (f32[4,8,128]{2,1,0:T(8,128)S(1)}, f32[4,8,128]{2,1,0:T(8,128)S(1)}, u32[]{:S(2)}, u32[]{:S(2)}) collective-permute-start(f32[4,8,128]{2,1,0:T(8,128)S(1)} %mul.463), channel_id=1, source_target_pairs={{16,0},{32,16},{48,32},{64,48},{80,64},{96,80},{112,96},{128,112},... | collective-permute-start | bytes 49160 | tf_op jit(solution)/shard_map/ppermute | solution.py:31
  301.2 5.9 %collective-permute-start.12 = (f32[4,4,128]{2,1,0:T(4,128)S(1)}, f32[4,4,128]{2,1,0:T(4,128)S(1)}, u32[]{:S(2)}, u32[]{:S(2)}) collective-permute-start(f32[4,4,128]{2,1,0:T(4,128)S(1)} %get-tuple-element.272), channel_id=1, source_target_pairs={{0,1},{1,2},{2,3},{3,4},{4,5},{5,6},{6,7},{7,8},{8,9},{9,10},{10,1... | collective-permute-start | bytes 24584 | tf_op jit(solution)/shard_map/ppermute | solution.py:29
  304.4 5.0 %collective-permute-start.13 = (f32[4,4,128]{2,1,0:T(4,128)S(1)}, f32[4,4,128]{2,1,0:T(4,128)S(1)}, u32[]{:S(2)}, u32[]{:S(2)}) collective-permute-start(f32[4,4,128]{2,1,0:T(4,128)S(1)} %get-tuple-element.273), channel_id=1, source_target_pairs={{1,0},{2,1},{3,2},{4,3},{5,4},{6,5},{7,6},{8,7},{9,8},{10,9},{11,1... | collective-permute-start | bytes 24584 | tf_op jit(solution)/shard_map/ppermute | solution.py:31
